TPU v7x, 256 devices: a whole 4x4x8 slice. The times are simulated.
256 devices in a mesh: blk: 8 (over x, core), dev: 32 (over z, y).
Axes of the slice: x: 4, y: 4, z: 8, core: 2. Of those that a mesh axis runs over, the one named last changes fastest.
Arguments:
- echoes: bfloat16 [2, 4, 2048, 16384], P(None, None, ('blk', 'dev')), may hold values from -6 to 6
- range_phase: float32 [16384], replicated, may hold values from -3.140625 to 3.140625
- offsets: int32 [16384], P('dev'), may hold values from 0 to 56, as said below
- tap_weights: float32 [8, 384], replicated, may hold values from -2 to 2
- channel_mix: float32 [2, 4, 4, 384], replicated, may hold values from -2 to 2
- azimuth_filter: float32 [2, 4, 384], replicated, may hold values from -4 to 4
Outputs:
- focused_image: bfloat16 [2, 4, 2048, 16384], P(None, None, 'blk', 'dev')
Inputs may be any that keep to these rules, and one draw needn't show every extreme that they name: `offsets`: each range bin's offset lies between 0 and 56; some range bin has exactly 56.
All inputs are finite; a program needn't handle non-finite values.
Results may differ from a plain program's by a relative error of at most 0.0088.
Values may be sent and summed in bfloat16 or wider, within the bound.
No kernel may reach another device: no remote copies, remote signals or barrier semaphores. Data moves between devices by JAX's collectives and lax.ppermute only.
A program may use at most 128 MiB of HBM per device.

v0:
```python
import math
import jax
import jax.numpy as jnp
from jax import lax
from jax.sharding import PartitionSpec as P

R1 = 128
MARG = 64


def shifted(block, axis, distance):
    devices = range(lax.axis_size(axis))
    route = [(i - distance, i) for i in devices if i - distance in devices]
    return lax.ppermute(block, axis, route)


def phase_pair(row_count, col_count, length, direction, factor):
    product = (
        jnp.arange(row_count, dtype=jnp.int32)[:, None]
        * jnp.arange(col_count, dtype=jnp.int32)[None, :]
        % length
    )
    angle = product.astype(jnp.float32) * (direction * 2.0 * math.pi / length)
    return (jnp.cos(angle) * factor, jnp.sin(angle) * factor)


def complex_table(row_count, col_count, length, direction, factor):
    cosine, sine = phase_pair(row_count, col_count, length, direction, factor)
    upper = jnp.stack([cosine, -sine], axis=1)
    lower = jnp.stack([sine, cosine], axis=1)
    return jnp.stack([upper, lower]).astype(jnp.bfloat16)


def apply_table(table, data, part_dim, index_dim):
    return lax.dot_general(
        table, data, (((2, 3), (part_dim, index_dim)), ((), ())), preferred_element_type=jnp.float32
    )


def compress(echoes, range_phase):
    cosine = jnp.cos(range_phase)
    sine = jnp.sin(range_phase)
    real_in = echoes[0].astype(jnp.float32)
    imag_in = echoes[1].astype(jnp.float32)
    spectrum = jnp.stack(
        [real_in * cosine - imag_in * sine, real_in * sine + imag_in * cosine]
    ).astype(jnp.bfloat16)
    channels = spectrum.shape[1]
    pulses = spectrum.shape[2]
    range_bins = spectrum.shape[3]
    second = range_bins // R1
    spectrum = spectrum.reshape((2, channels, pulses, R1, second))
    section = apply_table(complex_table(R1, R1, R1, 1.0, 1.0), spectrum, 0, 3)
    twist_re, twist_im = phase_pair(R1, second, range_bins, 1.0, 1.0 / math.sqrt(range_bins))
    twist_re = twist_re[:, None, None, :]
    twist_im = twist_im[:, None, None, :]
    partial_terms = jnp.stack(
        [
            section[0] * twist_re - section[1] * twist_im,
            section[0] * twist_im + section[1] * twist_re,
        ]
    ).astype(jnp.bfloat16)
    result = apply_table(
        complex_table(second, second, second, 1.0, 1.0), partial_terms, 0, 4
    ).astype(jnp.bfloat16)
    return result.transpose(0, 3, 4, 1, 2).reshape((2, channels, pulses, range_bins))


def doppler(window):
    wide = window.shape[2]
    forward = complex_table(wide, wide, wide, -1.0, 1.0 / math.sqrt(wide))
    return apply_table(forward, window, 0, 2).astype(jnp.bfloat16)


def migrate(extended, offsets, tap_weights, block):
    tile = min(128, block)
    taps = tap_weights.shape[0]
    pieces = []
    for tile_index in range(block // tile):
        first = tile_index * tile
        rows_here = jnp.arange(tile, dtype=jnp.int32)
        target = rows_here + offsets[first : first + tile]
        columns = jnp.arange(tile + MARG, dtype=jnp.int32)
        tap_range = jnp.arange(taps, dtype=jnp.int32)
        onehot = (
            columns[None, None, :] == target[None, :, None] + tap_range[:, None, None]
        ).astype(jnp.bfloat16)
        window_part = extended[:, :, :, first : first + tile + MARG]
        picked = lax.dot_general(
            window_part, onehot, (((3,), (2,)), ((), ())), preferred_element_type=jnp.float32
        )
        total = jnp.zeros(picked.shape[:3] + (tile,), jnp.float32)
        for tap_index in range(taps):
            total = total + picked[:, :, :, tap_index] * tap_weights[tap_index][None, :, None, None]
        pieces.append(total)
    return jnp.concatenate(pieces, axis=3)


def body(echoes, range_phase, offsets, tap_weights, channel_mix, azimuth_filter):
    dev_count = lax.axis_size("dev")
    compressed = compress(echoes, range_phase)
    range_bins = compressed.shape[3]
    block = range_bins // dev_count
    turned = lax.all_to_all(compressed, "dev", split_axis=3, concat_axis=2, tiled=True)
    group_pulses = turned.shape[2]
    intersection = group_pulses // 2
    following = shifted(turned[:, :, :intersection], "blk", -1)
    spectra = doppler(jnp.concatenate([turned, following], axis=2))
    border = shifted(spectra[:, :, :, :MARG], "dev", -1)
    extended = jnp.concatenate([spectra, border], axis=3)
    wide = extended.shape[1]
    channels = extended.shape[2]
    moved = migrate(extended, offsets, tap_weights, block)
    mix_real = (
        azimuth_filter[0][:, None, :] * channel_mix[0]
        - azimuth_filter[1][:, None, :] * channel_mix[1]
    )
    mix_imag = (
        azimuth_filter[0][:, None, :] * channel_mix[1]
        + azimuth_filter[1][:, None, :] * channel_mix[0]
    )
    rows_real = []
    rows_imag = []
    for channel in range(channels):
        sum_real = jnp.zeros((wide, block), jnp.float32)
        sum_imag = jnp.zeros((wide, block), jnp.float32)
        for other_chan in range(channels):
            coef_real = mix_real[channel, other_chan][:, None]
            coef_imag = mix_imag[channel, other_chan][:, None]
            sum_real = (
                sum_real + coef_real * moved[0, :, other_chan] - coef_imag * moved[1, :, other_chan]
            )
            sum_imag = (
                sum_imag + coef_real * moved[1, :, other_chan] + coef_imag * moved[0, :, other_chan]
            )
        rows_real.append(sum_real)
        rows_imag.append(sum_imag)
    focused = jnp.stack([jnp.stack(rows_real, axis=1), jnp.stack(rows_imag, axis=1)]).astype(
        jnp.bfloat16
    )
    backward = complex_table(group_pulses, wide, wide, 1.0, 1.0 / math.sqrt(wide))
    image = apply_table(backward, focused, 0, 1).astype(jnp.bfloat16)
    return image.transpose(0, 2, 1, 3)


def solution(mesh):
    in_specs = (P(None, None, ("blk", "dev"), None), P(), P("dev"), P(), P(), P())
    out_specs = P(None, None, "blk", "dev")
    return jax.shard_map(body, mesh=mesh, in_specs=in_specs, out_specs=out_specs, check_vma=False)
```

profile of v0, /device:TPU:35, one launch (start us, length us, event | category | flops | bytes accessed | tf_op | source)
XLA Modules:
  0.0 278.3 jit_solution(915196148581060619)
XLA Ops:
  0.8 1.1 fusion.138
  1.9 2.2 fusion.88
  6.1 0.7 fusion.15
  6.8 24.4 %copy.105 = bf16[2,4,8,128,128]{2,1,0,4,3:T(4,128)(2,1)} copy(bf16[2,4,8,128,128]{4,3,2,1,0:T(8,128)(2,1)S(1)} %fusion.15) | data formatting | bytes 4194304 | tf_op jit(solution)/shard_map/reshape | solution.py:66
  31.2 39.5 %reshape.3041 = bf16[32,2,16384]{2,1,0:T(2,128)(2,1)} reshape(bf16[16384,2,4,8]{3,2,1,0:T(4,128)(2,1)} %bitcast.547) | data formatting | bytes 4194304
  70.8 10.9 %all-to-all-start = ((bf16[32,2,16384]{2,1,0:T(2,128)(2,1)}), bf16[32,2,16384]{2,1,0:T(2,128)(2,1)S(1)}, u32[]{:S(2)}, u32[]{:S(2)}) async-start(bf16[32,2,16384]{2,1,0:T(2,128)(2,1)} %reshape.3041), calls=%async_computation | async-start | bytes 4194304 | tf_op jit(solution)/shard_map/all_to_all | solution.py:104
  83.1 1.5 fusion.116
  84.7 2.3 fusion.106
  87.0 1.7 negate_convert_fusion.1
  88.7 2.6 negate_convert_fusion
  91.3 0.8 maximum_bitcast_fusion.16
  92.2 36.5 %all-to-all-done = bf16[32,2,16384]{2,1,0:T(2,128)(2,1)S(1)} async-done(((bf16[32,2,16384]{2,1,0:T(2,128)(2,1)}), bf16[32,2,16384]{2,1,0:T(2,128)(2,1)S(1)}, u32[]{:S(2)}, u32[]{:S(2)}) %all-to-all-start) | async-done | bytes 2097184 | tf_op jit(solution)/shard_map/all_to_all | solution.py:104
  128.6 40.6 %reshape.3042 = bf16[16384,2,4,8]{3,2,1,0:T(4,128)(2,1)} reshape(bf16[32,2,16384]{2,1,0:T(2,128)(2,1)S(1)} %all-to-all-done) | data formatting | bytes 4194304
  169.2 40.2 %copy.47 = bf16[2,4,8,32,512]{4,2,3,0,1:T(8,128)(2,1)S(1)} copy(bf16[2,4,8,32,512]{2,1,0,4,3:T(4,128)(2,1)} %bitcast.548) | data formatting | bytes 4194304 | tf_op jit(solution)/shard_map/all_to_all | solution.py:104
  209.6 6.1 %collective-permute-start = (bf16[2,4,128,512]{3,2,0,1:T(8,128)(2,1)S(1)}, bf16[2,4,128,512]{3,2,0,1:T(8,128)(2,1)S(1)}, u32[]{:S(2)}, u32[]{:S(2)}) collective-permute-start(bf16[2,4,128,512]{3,2,0,1:T(8,128)(2,1)S(1)} %slice.481), channel_id=1, source_target_pairs={{32,0},{64,32},{96,64},{128,96},{160,128},{192,160},{224,192},{33,... | collective-permute-start | bytes 3145736 | tf_op jit(solution)/shard_map/ppermute | solution.py:14
  217.1 11.9 %collective-permute-done = bf16[2,4,128,512]{3,2,0,1:T(8,128)(2,1)S(1)} collective-permute-done((bf16[2,4,128,512]{3,2,0,1:T(8,128)(2,1)S(1)}, bf16[2,4,128,512]{3,2,0,1:T(8,128)(2,1)S(1)}, u32[]{:S(2)}, u32[]{:S(2)}) %collective-permute-start) | collective-permute-done | bytes 1048608 | tf_op jit(solution)/shard_map/ppermute | solution.py:14
  229.0 4.4 %bitcast_convert_fusion = bf16[2,384,4,512]{3,1,2,0:T(8,128)(2,1)S(1)} fusion(bf16[2,4,128,512]{3,2,0,1:T(8,128)(2,1)S(1)} %collective-permute-done, bf16[2,4,256,512]{3,2,0,1:T(8,128)(2,1)} %bitcast.550, bf16[1,384,2,384]{3,1,2,0:T(8,128)(2,1)S(1)} %get-tuple-element.50, bf16[1,384,2,384]{3,1,2,0:T(8,128)(2,1)S(1)} %get-tuple-element.49), kind=kOutput, calls=%fused_computation.1 | convolution fusion | flops 2426142720 | bytes 7471104 | tf_op jit(solution)/shard_map/dot_general | solution.py:35
  233.5 1.0 slice.509
  234.5 2.1 copy.74
  236.6 4.4 %collective-permute-start.1 = (bf16[2,384,4,64]{1,3,2,0:T(8,128)(2,1)}, bf16[2,384,4,64]{1,3,2,0:T(8,128)(2,1)}, u32[]{:S(2)}, u32[]{:S(2)}) collective-permute-start(bf16[2,384,4,64]{1,3,2,0:T(8,128)(2,1)} %copy.74), channel_id=1, source_target_pairs={{1,0},{2,1},{3,2},{4,3},{5,4},{6,5},{7,6},{8,7},{9,8},{10,9},{11,1... | collective-permute-start | bytes 1179656 | tf_op jit(solution)/shard_map/ppermute | solution.py:14
  241.1 1.8 fusion.52
  242.9 1.8 fusion.68
  244.9 6.4 %fusion.84 = f32[2,384,4,8,128]{1,4,3,2,0:T(8,128)} fusion(bf16[2,384,4,512]{3,1,2,0:T(8,128)(2,1)S(1)} %bitcast_convert_fusion, s32[8,128]{1,0:T(8,128)S(1)} %copy-done.51), kind=kOutput, calls=%fused_computation.132 | convolution fusion | flops 1208156160 | bytes 14159872 | tf_op jit(solution)/shard_map/dot_general | solution.py:89
  251.3 2.3 fusion.38
  253.6 2.3 fusion.54
  255.9 2.8 %copy-done = f32[2,384,4,8,128]{1,4,3,2,0:T(8,128)S(1)} copy-done((f32[2,384,4,8,128]{1,4,3,2,0:T(8,128)S(1)}, f32[2,384,4,8,128]{1,4,3,2,0:T(8,128)}, u32[]{:S(2)}) %copy-start) | copy-done | bytes 12582936
  258.7 2.3 fusion.70
  261.0 2.2 copy.75
  263.2 3.0 %fusion.34 = f32[2,384,4,8,128]{1,4,2,0,3:T(8,128)S(1)} fusion(bf16[2,384,4,64]{3,1,2,0:T(8,128)(2,1)} %copy.75, bf16[2,384,4,512]{3,1,2,0:T(8,128)(2,1)S(1)} %bitcast_convert_fusion, s32[8,128]{1,0:T(8,128)S(1)} %iota_add_fusion), kind=kOutput, calls=%fused_computation.56 | convolution fusion | flops 1210515456 | bytes 16125952 | tf_op jit(solution)/shard_map/dot_general | solution.py:89
  266.3 1.1 fusion.19
  274.4 0.7 copy-done.5
  275.1 3.1 %fusion.10 = bf16[2,4,256,512]{3,2,1,0:T(8,128)(2,1)} fusion(bf16[1,384,4,512]{1,3,2,0:T(8,128)(2,1)S(1)} %maximum_bitcast_fusion.11, bf16[1,384,4,512]{1,3,2,0:T(8,128)(2,1)S(1)} %maximum_bitcast_fusion.10, bf16[1,256,2,384]{3,1,2,0:T(8,128)(2,1)S(1)} %copy-done.5, bf16[1,256,2,384]{3,1,2,0:T(8,128)(2,1)S(1)} %get-tuple-element.51), kind=kOutput, calls=%fused_computation.21 | convolution fusion | flops 1619525632 | bytes 6029312 | tf_op jit(solution)/shard_map/dot_general | solution.py:35
  (138 shorter events, 12.3 us)
Async XLA Ops:
  70.8 10.9 %copy-start.53 = (f32[2,4,384]{2,1,0:T(4,128)S(1)}, f32[2,4,384]{2,1,0:T(4,128)}, u32[]{:S(2)}) copy-start(f32[2,4,384]{2,1,0:T(4,128)} %param.11) | copy-start | bytes 36868
  70.8 11.0 %copy-start.18 = (f32[2,4,4,384]{3,2,1,0:T(4,128)S(1)}, f32[2,4,4,384]{3,2,1,0:T(4,128)}, u32[]{:S(2)}) copy-start(f32[2,4,4,384]{3,2,1,0:T(4,128)} %param.10) | copy-start | bytes 147460
  70.8 57.9 %all-to-all-start = ((bf16[32,2,16384]{2,1,0:T(2,128)(2,1)}), bf16[32,2,16384]{2,1,0:T(2,128)(2,1)S(1)}, u32[]{:S(2)}, u32[]{:S(2)}) async-start(bf16[32,2,16384]{2,1,0:T(2,128)(2,1)} %reshape.3041), calls=%async_computation | async-start | bytes 4194304 | tf_op jit(solution)/shard_map/all_to_all | solution.py:104
  209.5 7.0 %copy-start.4 = (bf16[2,4,8,32,512]{4,2,3,0,1:T(8,128)(2,1)}, bf16[2,4,8,32,512]{4,2,3,0,1:T(8,128)(2,1)S(1)}, u32[]{:S(2)}) copy-start(bf16[2,4,8,32,512]{4,2,3,0,1:T(8,128)(2,1)S(1)} %copy.47) | copy-start | bytes 6291460
  209.5 6.2 %copy-start.52 = (f32[8,384]{1,0:T(8,128)S(1)}, f32[8,384]{1,0:T(8,128)}, u32[]{:S(2)}) copy-start(f32[8,384]{1,0:T(8,128)} %param.9) | copy-start | bytes 36868
  209.5 7.0 %copy-start.54 = (s32[512]{0:T(512)S(1)}, s32[512]{0:T(512)}, u32[]{:S(2)}) copy-start(s32[512]{0:T(512)} %param.8) | copy-start | bytes 6148
  209.6 19.4 %collective-permute-start = (bf16[2,4,128,512]{3,2,0,1:T(8,128)(2,1)S(1)}, bf16[2,4,128,512]{3,2,0,1:T(8,128)(2,1)S(1)}, u32[]{:S(2)}, u32[]{:S(2)}) collective-permute-start(bf16[2,4,128,512]{3,2,0,1:T(8,128)(2,1)S(1)} %slice.481), channel_id=1, source_target_pairs={{32,0},{64,32},{96,64},{128,96},{160,128},{192,160},{224,192},{33,... | collective-permute-start | bytes 3145736 | tf_op jit(solution)/shard_map/ppermute | solution.py:14
  236.6 24.4 %collective-permute-start.1 = (bf16[2,384,4,64]{1,3,2,0:T(8,128)(2,1)}, bf16[2,384,4,64]{1,3,2,0:T(8,128)(2,1)}, u32[]{:S(2)}, u32[]{:S(2)}) collective-permute-start(bf16[2,384,4,64]{1,3,2,0:T(8,128)(2,1)} %copy.74), channel_id=1, source_target_pairs={{1,0},{2,1},{3,2},{4,3},{5,4},{6,5},{7,6},{8,7},{9,8},{10,9},{11,1... | collective-permute-start | bytes 1179656 | tf_op jit(solution)/shard_map/ppermute | solution.py:14
  242.9 1.9 copy-start.51
  244.8 6.5 %copy-start.6 = (f32[384]{0:T(512)S(1)}, f32[384]{0:T(512)}, u32[]{:S(2)}) copy-start(f32[384]{0:T(512)} %get-tuple-element.38) | copy-start | bytes 4612
  244.8 6.5 %copy-start.7 = (f32[384]{0:T(512)S(1)}, f32[384]{0:T(512)}, u32[]{:S(2)}) copy-start(f32[384]{0:T(512)} %get-tuple-element.39) | copy-start | bytes 4612
  244.8 6.5 %copy-start.8 = (f32[384]{0:T(512)S(1)}, f32[384]{0:T(512)}, u32[]{:S(2)}) copy-start(f32[384]{0:T(512)} %get-tuple-element.40) | copy-start | bytes 4612
  244.8 6.5 %copy-start.10 = (f32[384]{0:T(512)S(1)}, f32[384]{0:T(512)}, u32[]{:S(2)}) copy-start(f32[384]{0:T(512)} %get-tuple-element.41) | copy-start | bytes 4612
  244.8 6.5 %copy-start.12 = (f32[384]{0:T(512)S(1)}, f32[384]{0:T(512)}, u32[]{:S(2)}) copy-start(f32[384]{0:T(512)} %get-tuple-element.42) | copy-start | bytes 4612
  244.8 6.5 %copy-start.14 = (f32[384]{0:T(512)S(1)}, f32[384]{0:T(512)}, u32[]{:S(2)}) copy-start(f32[384]{0:T(512)} %get-tuple-element.43) | copy-start | bytes 4612
  244.8 6.5 %copy-start.16 = (f32[384]{0:T(512)S(1)}, f32[384]{0:T(512)}, u32[]{:S(2)}) copy-start(f32[384]{0:T(512)} %get-tuple-element.44) | copy-start | bytes 4612
  253.6 5.1 %copy-start = (f32[2,384,4,8,128]{1,4,3,2,0:T(8,128)S(1)}, f32[2,384,4,8,128]{1,4,3,2,0:T(8,128)}, u32[]{:S(2)}) copy-start(f32[2,384,4,8,128]{1,4,3,2,0:T(8,128)} %fusion.84) | copy-start | bytes 37748740
  263.2 3.0 %copy-start.9 = (f32[384]{0:T(512)S(1)}, f32[384]{0:T(512)}, u32[]{:S(2)}) copy-start(f32[384]{0:T(512)} %get-tuple-element.40) | copy-start | bytes 4612
  263.2 3.0 %copy-start.11 = (f32[384]{0:T(512)S(1)}, f32[384]{0:T(512)}, u32[]{:S(2)}) copy-start(f32[384]{0:T(512)} %get-tuple-element.41) | copy-start | bytes 4612
  263.2 3.0 %copy-start.13 = (f32[384]{0:T(512)S(1)}, f32[384]{0:T(512)}, u32[]{:S(2)}) copy-start(f32[384]{0:T(512)} %get-tuple-element.42) | copy-start | bytes 4612
  263.2 3.0 %copy-start.15 = (f32[384]{0:T(512)S(1)}, f32[384]{0:T(512)}, u32[]{:S(2)}) copy-start(f32[384]{0:T(512)} %get-tuple-element.43) | copy-start | bytes 4612
  263.2 3.0 %copy-start.17 = (f32[384]{0:T(512)S(1)}, f32[384]{0:T(512)}, u32[]{:S(2)}) copy-start(f32[384]{0:T(512)} %get-tuple-element.44) | copy-start | bytes 4612
  266.2 1.4 copy-start.1
  266.3 1.9 copy-start.2
  266.3 2.3 copy-start.3
  268.6 0.8 copy-start.37
  268.6 0.8 copy-start.38
  268.6 0.8 copy-start.47
  268.6 0.8 copy-start.48
  268.6 0.8 copy-start.49
  268.6 0.8 copy-start.50
  274.1 1.0 copy-start.5
  (26 other events, 17.8 us)
where the time goes:
time: 281 us; the launch traced here: 278 us
  local copies, waits for them, and re-layouts  159 us (57%)
  waiting for transfers between devices  48.4 us (17%)
  other arithmetic  26.1 us (9%)
  matrix products  22.1 us (8%)
  starting transfers between devices  21.4 us (8%)
    unnamed x112, local copies, waits for them, and re-layouts  85.8 us
    all_to_all x1, local copies, waits for them, and re-layouts, body(): lax.all_to_all(compressed, 'dev', split_axis=3, concat_axis=2, tiled=True)  40.2 us
    all_to_all x1, waiting for transfers between devices, body(): lax.all_to_all(compressed, 'dev', split_axis=3, concat_axis=2, tiled=True)  36.5 us
    reshape x1, local copies, waits for them, and re-layouts, compress(): result.transpose(0, 3, 4, 1, 2).reshape((2, channels, pulses, range_bins))  24.4 us
    dot_general x4, matrix products, migrate(): lax.dot_general(window_part, onehot, (((3,), (2,)), ((), ())), preferred_...  13.1 us
    another operation x15, other arithmetic  12.8 us
    ppermute x2, waiting for transfers between devices, shifted(): return lax.ppermute(block, axis, route)  11.9 us
    all_to_all x1, starting transfers between devices, body(): lax.all_to_all(compressed, 'dev', split_axis=3, concat_axis=2, tiled=True)  10.9 us
  transfers between devices with their start and end apart: 3, of which 2 were waited for; matrix products, arithmetic and copies ran while one was open for 10% of the time, Pallas kernels for 0%

commit v1 on v0

--- a/solution.py
+++ b/solution.py
@@ -6,6 +6,18 @@
 
 R1 = 128
 MARG = 64
+
+
+def point_words_in(t0, lane_axis):
+    return jnp.concatenate(
+        jax.lax.all_to_all(
+            jnp.stack(jnp.split(t0, jax.lax.axis_size(lane_axis), axis=3)),
+            concat_axis=0,
+            axis_name=lane_axis,
+            split_axis=0,
+        ),
+        axis=2,
+    )
 
 
 def shifted(block, axis, distance):
@@ -101,7 +113,7 @@
     compressed = compress(echoes, range_phase)
     range_bins = compressed.shape[3]
     block = range_bins // dev_count
-    turned = lax.all_to_all(compressed, "dev", split_axis=3, concat_axis=2, tiled=True)
+    turned = point_words_in(compressed, "dev")
     group_pulses = turned.shape[2]
     intersection = group_pulses // 2
     following = shifted(turned[:, :, :intersection], "blk", -1)

time: 281 us -> 157 us (0.56)
  local copies, waits for them, and re-layouts: 159 us -> 37.9 us
    unnamed x112 -> x139, local copies, waits for them, and re-layouts: 85.8 us -> 25.2 us
    all_to_all x1 -> x0, local copies, waits for them, and re-layouts: 40.2 us -> none  [body(): lax.all_to_all(compressed, 'dev', split_axis=3, concat_axis=2, tiled=True)]
    reshape x1, local copies, waits for them, and re-layouts: 24.4 us -> 2.82 us  [compress(): result.transpose(0, 3, 4, 1, 2).reshape((2, channels, pulses, range_bins))]
  transfers between devices with their start and end apart: 3 -> 3, of which waited for: 2 -> 2; matrix products, arithmetic and copies ran while one was open for 10% -> 18% of each run, Pallas kernels for 0% -> 0%
where the time goes in v1:
time: 157 us
  waiting for transfers between devices  48.6 us (31%)
  local copies, waits for them, and re-layouts  37.9 us (24%)
  other arithmetic  26.1 us (17%)
  matrix products  21.9 us (14%)
  starting transfers between devices  21.4 us (14%)
    all_to_all x1, waiting for transfers between devices, point_words_in(): jax.lax.all_to_all(jnp.stack(jnp.split(t0, jax.lax.axis_size(lane_axis),...  36.5 us
    unnamed x139, local copies, waits for them, and re-layouts  25.2 us
    dot_general x4, matrix products, migrate(): lax.dot_general(window_part, onehot, (((3,), (2,)), ((), ())), preferred_...  13.1 us
    another operation x15, other arithmetic  12.8 us
    ppermute x2, waiting for transfers between devices, shifted(): return lax.ppermute(block, axis, route)  12.2 us
    all_to_all x1, starting transfers between devices, point_words_in(): jax.lax.all_to_all(jnp.stack(jnp.split(t0, jax.lax.axis_size(lane_axis),...  10.9 us
    ppermute x2, starting transfers between devices, shifted(): return lax.ppermute(block, axis, route)  10.5 us
    dot_general x4, matrix products, apply_table(): lax.dot_general(table, data, (((2, 3), (part_dim, index_dim)), ((), ())),...  8.78 us
  transfers between devices with their start and end apart: 3, of which 2 were waited for; matrix products, arithmetic and copies ran while one was open for 18% of the time, Pallas kernels for 0%

profile of v1, /device:TPU:35, one launch (start us, length us, event | category | flops | bytes accessed | tf_op | source)
XLA Modules:
  0.0 156.7 jit_solution(14900577113274204156)
XLA Ops:
  0.8 1.1 fusion.138
  1.9 2.2 %fusion.88 = (bf16[4,8,128,128]{3,1,2,0:T(8,128)(2,1)S(1)}, bf16[4,8,128,128]{3,1,2,0:T(8,128)(2,1)S(1)}) fusion(f32[16384]{0:T(1024)S(1)} %get-tuple-element.54, f32[16384]{0:T(1024)S(1)} %get-tuple-element.53, bf16[2,4,8,16384]{3,2,1,0:T(8,128)(2,1)} %param.6), kind=kLoop, calls=%fused_computation.140 | loop fusion | flops 5242880 | bytes 4325376
  4.7 0.7 convolution_bitcast_fusion
  6.1 2.1 %fusion.15 = bf16[2,4,8,128,128]{4,3,2,1,0:T(8,128)(2,1)} fusion(bf16[1,128,2,128]{3,1,2,0:T(8,128)(2,1)S(1)} %get-tuple-element.58, bf16[1,128,2,128]{3,1,2,0:T(8,128)(2,1)S(1)} %get-tuple-element.57, bf16[1,128,4,8,128]{4,1,3,2,0:T(8,128)(2,1)S(1)} %get-tuple-element.46, bf16[1,128,4,8,128]{4,1,3,2,0:T(8,128)(2,1)S(1)} %get-tuple-element.45), kind=kOutput, calls=%fused_computation.31 | convolution fusion | flops 539230208 | bytes 4325376 | tf_op jit(solution)/shard_map/dot_general | solution.py:47
  8.2 2.8 %reshape.2987 = bf16[2,4,8,16384]{3,2,1,0:T(8,128)(2,1)S(1)} reshape(bf16[2,4,8,128,128]{4,3,2,1,0:T(8,128)(2,1)} %fusion.15) | data formatting | bytes 4194304 | tf_op jit(solution)/shard_map/reshape | solution.py:78
  31.3 10.9 %all-to-all-start = ((bf16[32,2,4,8,512]{4,3,2,1,0:T(8,128)(2,1)}), bf16[32,2,4,8,512]{4,3,2,1,0:T(8,128)(2,1)S(1)}, u32[]{:S(2)}, u32[]{:S(2)}) async-start(bf16[32,2,4,8,512]{4,3,2,1,0:T(8,128)(2,1)} %constant_dynamic-update-slice_fusion), calls=%async_computation | async-start | bytes 4194304 | tf_op jit(solution)/shard_map/all_to_all | solution.py:13
  42.9 0.7 slice_reduce_fusion.31
  43.6 1.5 fusion.116
  45.2 2.3 %fusion.106 = bf16[384,1,384]{2,0,1:T(8,128)(2,1)S(1)} fusion(), kind=kLoop, calls=%fused_computation.184 | loop fusion | flops 1622016 | bytes 294912 | tf_op jit(solution)/shard_map/convert.29
  47.5 1.7 %negate_convert_fusion.1 = (bf16[256,1,384]{2,0,1:T(8,128)(2,1)S(1)}, bf16[256,1,384]{2,0,1:T(8,128)(2,1)S(1)}) fusion(), kind=kLoop, calls=%fused_computation.193 | loop fusion | flops 1376256 | bytes 393216 | tf_op jit(solution)/shard_map/convert.41
  49.2 2.6 %negate_convert_fusion = (bf16[384,1,384]{2,0,1:T(8,128)(2,1)S(1)}, bf16[384,1,384]{2,0,1:T(8,128)(2,1)S(1)}) fusion(), kind=kLoop, calls=%fused_computation.177 | loop fusion | flops 2064384 | bytes 589824 | tf_op jit(solution)/shard_map/convert.33
  51.8 0.8 maximum_bitcast_fusion.16
  52.7 36.5 %all-to-all-done = bf16[32,2,4,8,512]{4,3,2,1,0:T(8,128)(2,1)S(1)} async-done(((bf16[32,2,4,8,512]{4,3,2,1,0:T(8,128)(2,1)}), bf16[32,2,4,8,512]{4,3,2,1,0:T(8,128)(2,1)S(1)}, u32[]{:S(2)}, u32[]{:S(2)}) %all-to-all-start) | async-done | bytes 2097184 | tf_op jit(solution)/shard_map/all_to_all | solution.py:13
  89.4 5.9 %collective-permute-start = (bf16[2,4,128,512]{3,2,0,1:T(8,128)(2,1)S(1)}, bf16[2,4,128,512]{3,2,0,1:T(8,128)(2,1)S(1)}, u32[]{:S(2)}, u32[]{:S(2)}) collective-permute-start(bf16[2,4,128,512]{3,2,0,1:T(8,128)(2,1)S(1)} %slice.481), channel_id=1, source_target_pairs={{32,0},{64,32},{96,64},{128,96},{160,128},{192,160},{224,192},{33,... | collective-permute-start | bytes 3145736 | tf_op jit(solution)/shard_map/ppermute | solution.py:26
  96.7 12.2 %collective-permute-done = bf16[2,4,128,512]{3,2,0,1:T(8,128)(2,1)S(1)} collective-permute-done((bf16[2,4,128,512]{3,2,0,1:T(8,128)(2,1)S(1)}, bf16[2,4,128,512]{3,2,0,1:T(8,128)(2,1)S(1)}, u32[]{:S(2)}, u32[]{:S(2)}) %collective-permute-start) | collective-permute-done | bytes 1048608 | tf_op jit(solution)/shard_map/ppermute | solution.py:26
  108.9 2.8 %bitcast_convert_fusion = bf16[2,384,4,512]{3,1,2,0:T(8,128)(2,1)S(1)} fusion(bf16[2,4,128,512]{3,2,0,1:T(8,128)(2,1)S(1)} %collective-permute-done, bf16[2,4,256,512]{3,2,0,1:T(8,128)(2,1)S(1)} %copy_bitcast_fusion, bf16[1,384,2,384]{3,1,2,0:T(8,128)(2,1)S(1)} %get-tuple-element.50, bf16[1,384,2,384]{3,1,2,0:T(8,128)(2,1)S(1)} %get-tuple-element.49), kind=kOutput, calls=%fused_computation.1 | convolution fusion | flops 2426142720 | bytes 7471104 | tf_op jit(solution)/shard_map/dot_general | solution.py:47
  111.7 1.0 slice.509
  112.7 2.1 %copy.73 = bf16[2,384,4,64]{1,3,2,0:T(8,128)(2,1)} copy(bf16[2,384,4,64]{3,1,2,0:T(8,128)(2,1)} %slice.509) | data formatting | bytes 786432 | tf_op jit(solution)/shard_map/slice | solution.py:121
  114.9 4.6 %collective-permute-start.1 = (bf16[2,384,4,64]{1,3,2,0:T(8,128)(2,1)}, bf16[2,384,4,64]{1,3,2,0:T(8,128)(2,1)}, u32[]{:S(2)}, u32[]{:S(2)}) collective-permute-start(bf16[2,384,4,64]{1,3,2,0:T(8,128)(2,1)} %copy.73), channel_id=1, source_target_pairs={{1,0},{2,1},{3,2},{4,3},{5,4},{6,5},{7,6},{8,7},{9,8},{10,9},{11,1... | collective-permute-start | bytes 1179656 | tf_op jit(solution)/shard_map/ppermute | solution.py:26
  119.5 1.8 %fusion.52 = f32[2,384,4,8,128]{1,4,2,0,3:T(8,128)S(1)} fusion(bf16[2,384,4,512]{3,1,2,0:T(8,128)(2,1)S(1)} %bitcast_convert_fusion, s32[8,128]{1,0:T(8,128)S(1)} %get-tuple-element.73), kind=kOutput, calls=%fused_computation.83 | convolution fusion | flops 1208156160 | bytes 14159872 | tf_op jit(solution)/shard_map/dot_general | solution.py:101
  121.4 1.8 %fusion.68 = f32[2,384,4,8,128]{1,4,2,0,3:T(8,128)S(1)} fusion(bf16[2,384,4,512]{3,1,2,0:T(8,128)(2,1)S(1)} %bitcast_convert_fusion, s32[8,128]{1,0:T(8,128)S(1)} %get-tuple-element.74), kind=kOutput, calls=%fused_computation.108 | convolution fusion | flops 1208156160 | bytes 14159872 | tf_op jit(solution)/shard_map/dot_general | solution.py:101
  123.3 6.4 %fusion.84 = f32[2,384,4,8,128]{1,4,3,2,0:T(8,128)} fusion(bf16[2,384,4,512]{3,1,2,0:T(8,128)(2,1)S(1)} %bitcast_convert_fusion, s32[8,128]{1,0:T(8,128)S(1)} %copy-done.50), kind=kOutput, calls=%fused_computation.133 | convolution fusion | flops 1208156160 | bytes 14159872 | tf_op jit(solution)/shard_map/dot_general | solution.py:101
  129.7 2.3 %fusion.38 = f32[2,384,4,128]{1,3,2,0:T(8,128)} fusion(f32[2,384,4,8,128]{1,4,2,0,3:T(8,128)S(1)} %fusion.52, f32[384]{0:T(512)S(1)} %copy-done.13, f32[384]{0:T(512)S(1)} %copy-done.15, f32[384]{0:T(512)S(1)} %copy-done.5, f32[384]{0:T(512)S(1)} %copy-done.6, f32[384]{0:T(512)S(1)} %copy-done.7, f32[384]{0:T(512)S(1)} %copy-done.9, f32[384]{0:T(512)S(1)} %copy-done.11, ...), kind=kLoop, calls=%fused_computation.61 | loop fusion | flops 5898240 | bytes 14168064 | tf_op jit(solution)/shard_map/add | solution.py:106
  132.0 2.3 %fusion.54 = f32[2,384,4,128]{1,3,2,0:T(8,128)} fusion(f32[2,384,4,8,128]{1,4,2,0,3:T(8,128)S(1)} %fusion.68, f32[384]{0:T(512)S(1)} %copy-done.13, f32[384]{0:T(512)S(1)} %copy-done.15, f32[384]{0:T(512)S(1)} %copy-done.5, f32[384]{0:T(512)S(1)} %copy-done.6, f32[384]{0:T(512)S(1)} %copy-done.7, f32[384]{0:T(512)S(1)} %copy-done.9, f32[384]{0:T(512)S(1)} %copy-done.11, ...), kind=kLoop, calls=%fused_computation.86 | loop fusion | flops 5898240 | bytes 14168064 | tf_op jit(solution)/shard_map/add | solution.py:106
  134.4 2.8 %copy-done = f32[2,384,4,8,128]{1,4,3,2,0:T(8,128)S(1)} copy-done((f32[2,384,4,8,128]{1,4,3,2,0:T(8,128)S(1)}, f32[2,384,4,8,128]{1,4,3,2,0:T(8,128)}, u32[]{:S(2)}) %copy-start) | copy-done | bytes 12582936
  137.2 2.3 %fusion.70 = f32[2,384,4,128]{1,3,2,0:T(8,128)} fusion(f32[2,384,4,8,128]{1,4,3,2,0:T(8,128)S(1)} %copy-done, f32[384]{0:T(512)S(1)} %copy-done.13, f32[384]{0:T(512)S(1)} %copy-done.15, f32[384]{0:T(512)S(1)} %copy-done.5, f32[384]{0:T(512)S(1)} %copy-done.6, f32[384]{0:T(512)S(1)} %copy-done.7, f32[384]{0:T(512)S(1)} %copy-done.9, f32[384]{0:T(512)S(1)} %copy-done.11, ...), kind=kLoop, calls=%fused_computation.111 | loop fusion | flops 5898240 | bytes 14168064 | tf_op jit(solution)/shard_map/add | solution.py:106
  139.5 2.2 %copy.74 = bf16[2,384,4,64]{3,1,2,0:T(8,128)(2,1)} copy(bf16[2,384,4,64]{1,3,2,0:T(8,128)(2,1)} %collective-permute-done.1) | data formatting | bytes 786432 | tf_op jit(solution)/shard_map/ppermute | solution.py:26
  141.6 3.0 %fusion.34 = f32[2,384,4,8,128]{1,4,2,0,3:T(8,128)S(1)} fusion(bf16[2,384,4,64]{3,1,2,0:T(8,128)(2,1)} %copy.74, bf16[2,384,4,512]{3,1,2,0:T(8,128)(2,1)S(1)} %bitcast_convert_fusion, s32[8,128]{1,0:T(8,128)S(1)} %iota_add_fusion), kind=kOutput, calls=%fused_computation.57 | convolution fusion | flops 1210515456 | bytes 16125952 | tf_op jit(solution)/shard_map/dot_general | solution.py:101
  144.7 1.1 fusion.19
  147.1 0.7 pad_maximum_fusion
  152.8 0.7 copy-done.4
  153.5 3.2 %fusion.10 = bf16[2,4,256,512]{3,2,1,0:T(8,128)(2,1)} fusion(bf16[1,384,4,512]{1,3,2,0:T(8,128)(2,1)S(1)} %maximum_bitcast_fusion.11, bf16[1,384,4,512]{1,3,2,0:T(8,128)(2,1)S(1)} %maximum_bitcast_fusion.10, bf16[1,256,2,384]{3,1,2,0:T(8,128)(2,1)S(1)} %copy-done.4, bf16[1,256,2,384]{3,1,2,0:T(8,128)(2,1)S(1)} %get-tuple-element.51), kind=kOutput, calls=%fused_computation.21 | convolution fusion | flops 1619525632 | bytes 6029312 | tf_op jit(solution)/shard_map/dot_general | solution.py:47
  (166 shorter events, 30.7 us)
Async XLA Ops:
  31.3 10.9 %copy-start.52 = (f32[2,4,384]{2,1,0:T(4,128)S(1)}, f32[2,4,384]{2,1,0:T(4,128)}, u32[]{:S(2)}) copy-start(f32[2,4,384]{2,1,0:T(4,128)} %param.11) | copy-start | bytes 36868
  31.3 11.0 %copy-start.17 = (f32[2,4,4,384]{3,2,1,0:T(4,128)S(1)}, f32[2,4,4,384]{3,2,1,0:T(4,128)}, u32[]{:S(2)}) copy-start(f32[2,4,4,384]{3,2,1,0:T(4,128)} %param.10) | copy-start | bytes 147460
  31.3 57.9 %all-to-all-start = ((bf16[32,2,4,8,512]{4,3,2,1,0:T(8,128)(2,1)}), bf16[32,2,4,8,512]{4,3,2,1,0:T(8,128)(2,1)S(1)}, u32[]{:S(2)}, u32[]{:S(2)}) async-start(bf16[32,2,4,8,512]{4,3,2,1,0:T(8,128)(2,1)} %constant_dynamic-update-slice_fusion), calls=%async_computation | async-start | bytes 4194304 | tf_op jit(solution)/shard_map/all_to_all | solution.py:13
  89.3 6.0 %copy-start.51 = (f32[8,384]{1,0:T(8,128)S(1)}, f32[8,384]{1,0:T(8,128)}, u32[]{:S(2)}) copy-start(f32[8,384]{1,0:T(8,128)} %param.9) | copy-start | bytes 36868
  89.3 6.7 %copy-start.53 = (s32[512]{0:T(512)S(1)}, s32[512]{0:T(512)}, u32[]{:S(2)}) copy-start(s32[512]{0:T(512)} %param.8) | copy-start | bytes 6148
  89.4 19.4 %collective-permute-start = (bf16[2,4,128,512]{3,2,0,1:T(8,128)(2,1)S(1)}, bf16[2,4,128,512]{3,2,0,1:T(8,128)(2,1)S(1)}, u32[]{:S(2)}, u32[]{:S(2)}) collective-permute-start(bf16[2,4,128,512]{3,2,0,1:T(8,128)(2,1)S(1)} %slice.481), channel_id=1, source_target_pairs={{32,0},{64,32},{96,64},{128,96},{160,128},{192,160},{224,192},{33,... | collective-permute-start | bytes 3145736 | tf_op jit(solution)/shard_map/ppermute | solution.py:26
  114.9 24.6 %collective-permute-start.1 = (bf16[2,384,4,64]{1,3,2,0:T(8,128)(2,1)}, bf16[2,384,4,64]{1,3,2,0:T(8,128)(2,1)}, u32[]{:S(2)}, u32[]{:S(2)}) collective-permute-start(bf16[2,384,4,64]{1,3,2,0:T(8,128)(2,1)} %copy.73), channel_id=1, source_target_pairs={{1,0},{2,1},{3,2},{4,3},{5,4},{6,5},{7,6},{8,7},{9,8},{10,9},{11,1... | collective-permute-start | bytes 1179656 | tf_op jit(solution)/shard_map/ppermute | solution.py:26
  121.3 1.9 %copy-start.50 = (s32[8,128]{1,0:T(8,128)S(1)}, s32[8,128]{1,0:T(8,128)}, u32[]{:S(2)}) copy-start(s32[8,128]{1,0:T(8,128)} %iota_add_fusion.3) | copy-start | bytes 12292
  123.2 6.5 %copy-start.5 = (f32[384]{0:T(512)S(1)}, f32[384]{0:T(512)}, u32[]{:S(2)}) copy-start(f32[384]{0:T(512)} %get-tuple-element.38) | copy-start | bytes 4612
  123.2 6.5 %copy-start.6 = (f32[384]{0:T(512)S(1)}, f32[384]{0:T(512)}, u32[]{:S(2)}) copy-start(f32[384]{0:T(512)} %get-tuple-element.39) | copy-start | bytes 4612
  123.2 6.5 %copy-start.7 = (f32[384]{0:T(512)S(1)}, f32[384]{0:T(512)}, u32[]{:S(2)}) copy-start(f32[384]{0:T(512)} %get-tuple-element.40) | copy-start | bytes 4612
  123.2 6.5 %copy-start.9 = (f32[384]{0:T(512)S(1)}, f32[384]{0:T(512)}, u32[]{:S(2)}) copy-start(f32[384]{0:T(512)} %get-tuple-element.41) | copy-start | bytes 4612
  123.3 6.5 %copy-start.11 = (f32[384]{0:T(512)S(1)}, f32[384]{0:T(512)}, u32[]{:S(2)}) copy-start(f32[384]{0:T(512)} %get-tuple-element.42) | copy-start | bytes 4612
  123.3 6.5 %copy-start.13 = (f32[384]{0:T(512)S(1)}, f32[384]{0:T(512)}, u32[]{:S(2)}) copy-start(f32[384]{0:T(512)} %get-tuple-element.43) | copy-start | bytes 4612
  123.3 6.5 %copy-start.15 = (f32[384]{0:T(512)S(1)}, f32[384]{0:T(512)}, u32[]{:S(2)}) copy-start(f32[384]{0:T(512)} %get-tuple-element.44) | copy-start | bytes 4612
  132.0 5.1 %copy-start = (f32[2,384,4,8,128]{1,4,3,2,0:T(8,128)S(1)}, f32[2,384,4,8,128]{1,4,3,2,0:T(8,128)}, u32[]{:S(2)}) copy-start(f32[2,384,4,8,128]{1,4,3,2,0:T(8,128)} %fusion.84) | copy-start | bytes 37748740
  141.6 3.0 %copy-start.8 = (f32[384]{0:T(512)S(1)}, f32[384]{0:T(512)}, u32[]{:S(2)}) copy-start(f32[384]{0:T(512)} %get-tuple-element.40) | copy-start | bytes 4612
  141.6 3.0 %copy-start.10 = (f32[384]{0:T(512)S(1)}, f32[384]{0:T(512)}, u32[]{:S(2)}) copy-start(f32[384]{0:T(512)} %get-tuple-element.41) | copy-start | bytes 4612
  141.6 3.0 %copy-start.12 = (f32[384]{0:T(512)S(1)}, f32[384]{0:T(512)}, u32[]{:S(2)}) copy-start(f32[384]{0:T(512)} %get-tuple-element.42) | copy-start | bytes 4612
  141.6 3.0 %copy-start.14 = (f32[384]{0:T(512)S(1)}, f32[384]{0:T(512)}, u32[]{:S(2)}) copy-start(f32[384]{0:T(512)} %get-tuple-element.43) | copy-start | bytes 4612
  141.6 3.0 %copy-start.16 = (f32[384]{0:T(512)S(1)}, f32[384]{0:T(512)}, u32[]{:S(2)}) copy-start(f32[384]{0:T(512)} %get-tuple-element.44) | copy-start | bytes 4612
  144.7 1.4 copy-start.1
  144.7 1.9 %copy-start.2 = (f32[2,384,4,128]{1,3,2,0:T(8,128)S(1)}, f32[2,384,4,128]{1,3,2,0:T(8,128)}, u32[]{:S(2)}) copy-start(f32[2,384,4,128]{1,3,2,0:T(8,128)} %fusion.54) | copy-start | bytes 4718596
  144.7 2.3 %copy-start.3 = (f32[2,384,4,128]{1,3,2,0:T(8,128)S(1)}, f32[2,384,4,128]{1,3,2,0:T(8,128)}, u32[]{:S(2)}) copy-start(f32[2,384,4,128]{1,3,2,0:T(8,128)} %fusion.70) | copy-start | bytes 4718596
  147.0 0.7 copy-start.35
  147.0 0.8 copy-start.36
  147.0 0.8 copy-start.37
  147.0 0.8 copy-start.46
  147.1 0.8 copy-start.47
  147.1 0.8 copy-start.48
  147.1 0.8 copy-start.49
  152.5 1.0 copy-start.4
  (25 other events, 16.7 us)
